TPU v7x, 32 devices: a whole 2x2x4 slice. The times are simulated.
32 devices in a mesh: leaf: 8 (over z, y), case: 4 (over x, core).
Axes of the slice: x: 2, y: 2, z: 4, core: 2. Of those that a mesh axis runs over, the one named last changes fastest.
Arguments:
- features: bfloat16 [8, 16384, 128], P('case', 'leaf'), may hold values from -6 to 6
- cotangent: bfloat16 [8, 16384, 128], P('case', 'leaf'), may hold values from -6 to 6
- kernel_blocks: bfloat16 [128, 12, 128, 128], P('leaf'), may hold values from -0.15625 to 0.15625
- near_pairs: int32 [128, 12], P('leaf'), may hold values from 0 to 127, as said below
- leaf_basis: bfloat16 [64, 16384], P(None, 'leaf'), may hold values from -0.125 to 0.125
- w_near: bfloat16 [128, 128], replicated, may hold values from -0.5 to 0.5
- w_far: bfloat16 [128, 128], replicated, may hold values from -0.5 to 0.5
- translations: float32 [3, 64, 64], replicated, may hold values from -0.75 to 0.75
Outputs:
- output: bfloat16 [8, 16384, 128], P('case', 'leaf')
- grad_features: bfloat16 [8, 16384, 128], P('case', 'leaf')
- grad_near: float32 [128, 128], replicated
- grad_far: float32 [128, 128], replicated
Inputs may be any that keep to these rules, and one draw needn't show every extreme that they name: `near_pairs`: A target block held by one index of leaf names blocks of that index, or blocks at most 8 places beyond its first or last block; on every index both of these farthest blocks occur where they exist; 0 and 127 both occur.
All inputs are finite; a program needn't handle non-finite values.
Results may differ from a plain program's by a relative error of at most 0.0085.
Values may be sent and summed in bfloat16 or wider, within the bound.
No kernel may reach another device: no remote copies, remote signals or barrier semaphores. Data moves between devices by JAX's collectives and lax.ppermute only.
A program may use at most 128 MiB of HBM per device.

v0:
```python
import math
import jax
import jax.numpy as jnp
from jax import lax
from jax.sharding import PartitionSpec as P


def partner(shard, axis, apart):
    return lax.ppermute(shard, axis, [(i, i ^ 1 << apart) for i in range(lax.axis_size(axis))])


def with_halo(cells, sides, width):
    for axis, dim in sides:
        count = lax.axis_size(axis)
        ends = count - 1
        head = lax.slice_in_dim(cells, 0, width, axis=dim)
        tail = lax.slice_in_dim(cells, cells.shape[dim] - width, cells.shape[dim], axis=dim)
        cells = jnp.concatenate(
            [
                lax.ppermute(tail, axis, [(i, (i + 1) % count) for i in range(ends)]),
                cells,
                lax.ppermute(head, axis, [((i + 1) % count, i) for i in range(ends)]),
            ],
            axis=dim,
        )
    return cells


def shifted(value, axis, steps):
    count = lax.axis_size(axis)
    leading, last = (max(0, -steps), min(count, count - steps))
    return lax.ppermute(value, axis, [(source, source + steps) for source in range(leading, last)])


def apply_level(matrix, sibling, flipped):
    if flipped:
        return jnp.einsum("sr,asc->arc", matrix, sibling, precision=lax.Precision.HIGHEST)
    return jnp.einsum("rs,asc->arc", matrix, sibling, precision=lax.Precision.HIGHEST)


def expand(own_value, translations, flipped):
    depth_count = lax.axis_size("leaf").bit_length() - 1
    summed = jnp.zeros(own_value.shape, jnp.float32)
    node_value = own_value
    for height in range(depth_count):
        sibling = partner(node_value, "leaf", height)
        summed = summed + apply_level(translations[height], sibling, flipped)
        node_value = node_value + sibling
    return summed


def on_device(
    features, cotangent, kernel_blocks, near_pairs, leaf_basis, w_near, w_far, translations
):
    cases_here, points_here, width = features.shape
    blocks_here, pair_count, block_rows = (
        kernel_blocks.shape[0],
        kernel_blocks.shape[1],
        kernel_blocks.shape[2],
    )
    position = lax.axis_index("leaf")
    extended = with_halo(features, (("leaf", 1),), points_here)
    span_blocks = blocks_here + 2 * blocks_here
    ext_blocks = extended.reshape(cases_here, span_blocks, block_rows, width)
    local_ids = (near_pairs - (position * blocks_here - blocks_here)).reshape(-1)
    picked = jnp.take(ext_blocks, local_ids, axis=1).reshape(
        cases_here, blocks_here, pair_count, block_rows, width
    )
    near_sum = jnp.einsum(
        "bkij,abkjc->abic", kernel_blocks, picked, preferred_element_type=jnp.float32
    )
    near_bf = near_sum.reshape(cases_here, points_here, width).astype(jnp.bfloat16)
    summary = jnp.einsum("rp,apc->arc", leaf_basis, features, preferred_element_type=jnp.float32)
    expansion = expand(summary, translations, False)
    exp_bf = expansion.astype(jnp.bfloat16)
    far_coeff = jnp.einsum("arc,cd->ard", exp_bf, w_far, preferred_element_type=jnp.float32).astype(
        jnp.bfloat16
    )
    far_field = jnp.einsum("rp,ard->apd", leaf_basis, far_coeff, preferred_element_type=jnp.float32)
    mixed = (
        jnp.einsum("apc,cd->apd", near_bf, w_near, preferred_element_type=jnp.float32) + far_field
    )
    output = jax.nn.gelu(mixed).astype(jnp.bfloat16)
    _, pullback = jax.vjp(jax.nn.gelu, mixed)
    slope = pullback(cotangent.astype(jnp.float32))[0].astype(jnp.bfloat16)
    projected = jnp.einsum(
        "rp,apc->arc", leaf_basis, slope, preferred_element_type=jnp.float32
    ).astype(jnp.bfloat16)
    back_coeff = jnp.einsum("arc,dc->ard", projected, w_far, preferred_element_type=jnp.float32)
    back_exp = expand(back_coeff, translations, True)
    back_far = jnp.einsum(
        "rp,arc->apc", leaf_basis, back_exp.astype(jnp.bfloat16), preferred_element_type=jnp.float32
    )
    back_near = jnp.einsum("apc,dc->apd", slope, w_near, preferred_element_type=jnp.float32).astype(
        jnp.bfloat16
    )
    back_blocks = back_near.reshape(cases_here, blocks_here, block_rows, width)
    contrib = jnp.einsum(
        "bkij,abic->bkajc", kernel_blocks, back_blocks, preferred_element_type=jnp.float32
    )
    contrib = contrib.reshape(blocks_here * pair_count, cases_here, block_rows, width)
    landed = jax.ops.segment_sum(contrib, local_ids, num_segments=span_blocks)
    left_part = landed[:blocks_here]
    middle_part = landed[blocks_here : blocks_here + blocks_here]
    right_part = landed[blocks_here + blocks_here :]
    from_next = shifted(left_part.astype(jnp.bfloat16), "leaf", -1).astype(left_part.dtype)
    from_prev = shifted(right_part.astype(jnp.bfloat16), "leaf", 1).astype(right_part.dtype)
    gathered_near = middle_part + from_next + from_prev
    back_near_sum = gathered_near.transpose(1, 0, 2, 3).reshape(cases_here, points_here, width)
    grad_features = (back_near_sum + back_far).astype(jnp.bfloat16)
    scale = 1.0 / math.sqrt(
        cases_here * lax.axis_size("case") * points_here * lax.axis_size("leaf")
    )
    near_term = (
        jnp.einsum("apc,apd->cd", near_bf, slope, preferred_element_type=jnp.float32) * scale
    )
    far_term = (
        jnp.einsum("arc,ard->cd", exp_bf, projected, preferred_element_type=jnp.float32) * scale
    )
    grad_near, grad_far = lax.psum((near_term, far_term), ("leaf", "case"))
    return (output, grad_features, grad_near, grad_far)


def solution(mesh):
    return jax.shard_map(
        on_device,
        mesh=mesh,
        in_specs=(
            P("case", "leaf", None),
            P("case", "leaf", None),
            P("leaf", None, None, None),
            P("leaf", None),
            P(None, "leaf"),
            P(),
            P(),
            P(),
        ),
        out_specs=(P("case", "leaf", None), P("case", "leaf", None), P(), P()),
        check_vma=False,
    )
```

profile of v0, /device:TPU:0, one launch (start us, length us, event | category | flops | bytes accessed | tf_op | source)
XLA Modules:
  0.0 359.6 jit_solution(16556230183017255712)
XLA Ops:
  7.2 5.1 %collective-permute-start = (bf16[2,2048,128]{2,1,0:T(8,128)(2,1)}, bf16[2,2048,128]{2,1,0:T(8,128)(2,1)S(1)}, u32[]{:S(2)}, u32[]{:S(2)}) collective-permute-start(bf16[2,2048,128]{2,1,0:T(8,128)(2,1)} %param.8), channel_id=1, source_target_pairs={{0,4},{4,8},{8,12},{12,16},{16,20},{20,24},{24,28},{1,5},{5,9},{9,... | collective-permute-start | bytes 3145736 | tf_op jit(solution)/shard_map/ppermute | solution.py:20
  12.3 1.3 collective-permute-start.1
  13.6 1.5 convolution_bitcast_fusion.3
  15.2 2.7 collective-permute-start.2
  18.8 39.9 %collective-permute-done.2 = f32[2,64,128]{2,1,0:T(8,128)S(1)} collective-permute-done((f32[2,64,128]{2,1,0:T(8,128)S(1)}, f32[2,64,128]{2,1,0:T(8,128)S(1)}, u32[]{:S(2)}, u32[]{:S(2)}) %collective-permute-start.2) | collective-permute-done | bytes 65568 | tf_op jit(solution)/shard_map/ppermute | solution.py:9
  58.7 3.5 collective-permute-start.3
  62.3 2.3 collective-permute-done.3
  64.5 3.1 collective-permute-start.4
  67.6 1.0 fusion.50
  68.6 1.3 collective-permute-done.4
  69.9 1.0 fusion.46
  71.1 1.0 copy-done.2
  72.0 2.0 pad_maximum_fusion
  74.0 8.2 %gather_fusion = bf16[192,2,128,128]{3,2,1,0:T(8,128)(2,1)} fusion(bf16[2,48,128,128]{3,2,1,0:T(8,128)(2,1)S(1)} %bitcast.123, s32[1024]{0:T(1024)S(1)} %pad_clamp_fusion), kind=kCustom, calls=%fused_computation | custom fusion | bytes 25166592 | tf_op jit(solution)/shard_map/jit(_take)/gather | solution.py:66
  82.2 6.5 %copy.24 = bf16[2,192,128,128]{3,2,1,0:T(8,128)(2,1)S(1)} copy(bf16[2,192,128,128]{3,2,0,1:T(8,128)(2,1)} %bitcast.124) | data formatting | bytes 25165824 | tf_op jit(solution)/shard_map/jit(_take)/gather | solution.py:66
  88.7 5.5 %fusion.21 = bf16[2,16,128,128]{3,2,0,1:T(8,128)(2,1)} fusion(bf16[16,12,128,128]{3,2,1,0:T(8,128)(2,1)} %param.10, bf16[2,16,12,128,128]{4,3,2,1,0:T(8,128)(2,1)S(1)} %bitcast.125, pred[16,12]{1,0:T(8,128)(4,1)S(1)} %get-tuple-element.18), kind=kOutput, calls=%fused_computation.33 | convolution fusion | flops 1617428480 | bytes 19923136 | tf_op jit(solution)/shard_map/bkij,abkjc->abic/dot_general | solution.py:69
  94.2 1.3 copy.26
  95.6 1.8 fusion.55
  97.3 5.0 %fusion.7 = (bf16[2,2048,128]{2,1,0:T(8,128)(2,1)S(1)}, bf16[2,2048,128]{2,1,0:T(8,128)(2,1)}) fusion(bf16[2,2048,128]{2,1,0:T(8,128)(2,1)} %param.9, f32[2,2048,128]{2,1,0:T(8,128)} %fusion.55, bf16[64,2048]{1,0:T(8,128)(2,1)S(1)} %copy-done, bf16[2,64,128]{2,1,0:T(8,128)(2,1)S(1)} %fusion.34, bf16[128,128]{1,0:T(8,128)(2,1)S(1)} %copy-done.8), kind=kOutput, calls=%fused_computation.19 | convolution fusion | flops 83902464 | bytes 5570560 | tf_op jit(solution)/shard_map/rp,ard->apd/dot_general | solution.py:79
  103.0 0.8 fusion.40
  103.8 1.0 collective-permute-start.7
  104.8 12.9 %convolution_bitcast_fusion = f32[16,12,2,128,128]{3,4,1,2,0:T(8,128)} fusion(bf16[16,12,128,128]{3,2,1,0:T(8,128)(2,1)} %param.10, bf16[2,16,128,128,1]{3,2,1,0,4:T(8,128)(2,1)S(1)} %bitcast.128), kind=kOutput, calls=%fused_computation.5 | convolution fusion | flops 1610612736 | bytes 32505856 | tf_op jit(solution)/shard_map/bkij,abic->bkajc/dot_general | solution.py:98
  117.7 24.7 %copy.29 = f32[16,12,2,128,128]{4,3,2,1,0:T(8,128)} copy(f32[16,12,2,128,128]{3,4,1,2,0:T(8,128)} %convolution_bitcast_fusion) | data formatting | bytes 50331648 | tf_op jit(solution)/shard_map/bkij,abic->bkajc/transpose | solution.py:98
  142.4 3.5 broadcast_in_dim.15
  145.9 56.4 %scatter_fusion = f32[48,2,128,128]{3,2,1,0:T(8,128)} fusion(f32[48,2,128,128]{3,2,1,0:T(8,128)} %broadcast_in_dim.15, s32[192]{0:T(256)S(1)} %reshape.77, f32[192,2,128,128]{3,2,1,0:T(8,128)} %bitcast.122), kind=kCustom, calls=%fused_computation.1 | custom fusion | flops 6291456 | bytes 75498240 | tf_op jit(solution)/shard_map/scatter-add | solution.py:102
  202.3 3.5 convert.4
  205.8 1.1 fusion.63
  206.9 1.1 fusion.27
  208.0 1.3 collective-permute-start.5
  209.3 5.5 %collective-permute-start.6 = (bf16[16,2,128,128]{3,2,1,0:T(8,128)(2,1)S(1)}, bf16[16,2,128,128]{3,2,1,0:T(8,128)(2,1)}, u32[]{:S(2)}, u32[]{:S(2)}) collective-permute-start(bf16[16,2,128,128]{3,2,1,0:T(8,128)(2,1)S(1)} %get-tuple-element.21), channel_id=1, source_target_pairs={{0,4},{4,8},{8,12},{12,16},{16,20},{20,24},{24,28},{1,5},{5,9},{9,... | collective-permute-start | bytes 3145736 | tf_op jit(solution)/shard_map/ppermute | solution.py:32
  214.9 0.9 add.91
  215.7 1.0 collective-permute-start.8
  216.8 0.8 fusion.26
  217.6 17.8 %collective-permute-done.8 = f32[2,64,128]{2,1,0:T(8,128)S(1)} collective-permute-done((f32[2,64,128]{2,1,0:T(8,128)S(1)}, f32[2,64,128]{2,1,0:T(8,128)S(1)}, u32[]{:S(2)}, u32[]{:S(2)}) %collective-permute-start.8) | collective-permute-done | bytes 65568 | tf_op jit(solution)/shard_map/ppermute | solution.py:9
  235.4 3.8 %collective-permute-start.9 = (f32[2,64,128]{2,1,0:T(8,128)S(1)}, f32[2,64,128]{2,1,0:T(8,128)S(1)}, u32[]{:S(2)}, u32[]{:S(2)}) collective-permute-start(f32[2,64,128]{2,1,0:T(8,128)S(1)} %add.93), channel_id=1, source_target_pairs={{0,16},{4,20},{8,24},{12,28},{16,0},{20,4},{24,8},{28,12},{1,17},{... | collective-permute-start | bytes 196616 | tf_op jit(solution)/shard_map/ppermute | solution.py:9
  239.5 2.0 collective-permute-done.9
  241.7 1.1 fusion.33
  242.8 1.8 convolution_bitcast_fusion.1
  244.6 1.0 copy-done.3
  245.6 9.9 %collective-permute-done.6 = bf16[16,2,128,128]{3,2,1,0:T(8,128)(2,1)} collective-permute-done((bf16[16,2,128,128]{3,2,1,0:T(8,128)(2,1)S(1)}, bf16[16,2,128,128]{3,2,1,0:T(8,128)(2,1)}, u32[]{:S(2)}, u32[]{:S(2)}) %collective-permute-start.6) | collective-permute-done | bytes 1048608 | tf_op jit(solution)/shard_map/ppermute | solution.py:32
  255.5 2.6 fusion.16
  258.1 2.0 copy.30
  260.1 2.8 reshape.66
  263.0 1.8 add_convert_fusion
  264.8 1.3 copy.35
  266.1 83.7 %all-reduce.3.cloned.1.call-done = (f32[128,128]{1,0:T(8,128)}, f32[128,128]{1,0:T(8,128)}) async-done(((f32[128,128]{1,0:T(8,128)}, f32[128,128]{1,0:T(8,128)}), (f32[128,128]{1,0:T(8,128)}, f32[128,128]{1,0:T(8,128)})) %all-reduce.3.cloned.1.call-update) | async-done | bytes 131088 | tf_op jit(solution)/shard_map/psum | solution.py:120
  349.8 1.5 copy.60
  351.3 1.5 copy.61
  (35 shorter events, 2.4 us)
Async XLA Ops:
  7.2 6.5 %copy-start = (bf16[64,2048]{1,0:T(8,128)(2,1)S(1)}, bf16[64,2048]{1,0:T(8,128)(2,1)}, u32[]{:S(2)}) copy-start(bf16[64,2048]{1,0:T(8,128)(2,1)} %param.12) | copy-start | bytes 786436
  7.2 63.6 %copy-start.4 = (f32[3,64,64]{2,1,0:T(8,128)S(1)}, f32[3,64,64]{2,1,0:T(8,128)}, u32[]{:S(2)}) copy-start(f32[3,64,64]{2,1,0:T(8,128)} %param.15) | copy-start | bytes 147460
  7.2 342.6 %all-reduce.3.cloned.1.call-start = ((), (), s32[]{:S(2)}) async-start(), calls=%async_computation | async-start | bytes 262144 | tf_op jit(solution)/shard_map/psum | solution.py:120
  7.2 63.8 %collective-permute-start = (bf16[2,2048,128]{2,1,0:T(8,128)(2,1)}, bf16[2,2048,128]{2,1,0:T(8,128)(2,1)S(1)}, u32[]{:S(2)}, u32[]{:S(2)}) collective-permute-start(bf16[2,2048,128]{2,1,0:T(8,128)(2,1)} %param.8), channel_id=1, source_target_pairs={{0,4},{4,8},{8,12},{12,16},{16,20},{20,24},{24,28},{1,5},{5,9},{9,... | collective-permute-start | bytes 3145736 | tf_op jit(solution)/shard_map/ppermute | solution.py:20
  12.3 59.7 %collective-permute-start.1 = (bf16[2,2048,128]{2,1,0:T(8,128)(2,1)}, bf16[2,2048,128]{2,1,0:T(8,128)(2,1)}, u32[]{:S(2)}, u32[]{:S(2)}) collective-permute-start(bf16[2,2048,128]{2,1,0:T(8,128)(2,1)} %param.8), channel_id=1, source_target_pairs={{4,0},{8,4},{12,8},{16,12},{20,16},{24,20},{28,24},{5,1},{9,5},{13... | collective-permute-start | bytes 3145736 | tf_op jit(solution)/shard_map/ppermute | solution.py:22
  15.2 43.6 %collective-permute-start.2 = (f32[2,64,128]{2,1,0:T(8,128)S(1)}, f32[2,64,128]{2,1,0:T(8,128)S(1)}, u32[]{:S(2)}, u32[]{:S(2)}) collective-permute-start(f32[2,64,128]{2,1,0:T(8,128)S(1)} %convolution_bitcast_fusion.3), channel_id=1, source_target_pairs={{0,4},{4,0},{8,12},{12,8},{16,20},{20,16},{24,28},{28,24},{1,5},{5... | collective-permute-start | bytes 196616 | tf_op jit(solution)/shard_map/ppermute | solution.py:9
  58.7 5.8 %collective-permute-start.3 = (f32[2,64,128]{2,1,0:T(8,128)S(1)}, f32[2,64,128]{2,1,0:T(8,128)S(1)}, u32[]{:S(2)}, u32[]{:S(2)}) collective-permute-start(f32[2,64,128]{2,1,0:T(8,128)S(1)} %add.82), channel_id=1, source_target_pairs={{0,8},{4,12},{8,0},{12,4},{16,24},{20,28},{24,16},{28,20},{1,9},{5... | collective-permute-start | bytes 196616 | tf_op jit(solution)/shard_map/ppermute | solution.py:9
  64.5 5.3 %collective-permute-start.4 = (f32[2,64,128]{2,1,0:T(8,128)S(1)}, f32[2,64,128]{2,1,0:T(8,128)S(1)}, u32[]{:S(2)}, u32[]{:S(2)}) collective-permute-start(f32[2,64,128]{2,1,0:T(8,128)S(1)} %add.84), channel_id=1, source_target_pairs={{0,16},{4,20},{8,24},{12,28},{16,0},{20,4},{24,8},{28,12},{1,17},{... | collective-permute-start | bytes 196616 | tf_op jit(solution)/shard_map/ppermute | solution.py:9
  71.0 26.3 %copy-start.6 = (bf16[2,64,128]{2,1,0:T(8,128)(2,1)}, bf16[2,64,128]{2,1,0:T(8,128)(2,1)S(1)}, u32[]{:S(2)}) copy-start(bf16[2,64,128]{2,1,0:T(8,128)(2,1)S(1)} %fusion.34) | copy-start | bytes 98308
  71.1 1.0 copy-start.2
  94.2 1.3 copy-start.5
  95.5 1.8 copy-start.8
  103.8 111.0 %collective-permute-start.7 = (f32[2,64,128]{2,1,0:T(8,128)}, f32[2,64,128]{2,1,0:T(8,128)}, u32[]{:S(2)}, u32[]{:S(2)}) collective-permute-start(f32[2,64,128]{2,1,0:T(8,128)} %fusion.40), channel_id=1, source_target_pairs={{0,4},{4,0},{8,12},{12,8},{16,20},{20,16},{24,28},{28,24},{1,5},{5... | collective-permute-start | bytes 196616 | tf_op jit(solution)/shard_map/ppermute | solution.py:9
  206.9 9.9 %copy-start.7 = (bf16[2,64,128]{2,1,0:T(8,128)(2,1)S(1)}, bf16[2,64,128]{2,1,0:T(8,128)(2,1)}, u32[]{:S(2)}) copy-start(bf16[2,64,128]{2,1,0:T(8,128)(2,1)} %copy-done.6) | copy-start | bytes 98308
  208.0 36.6 %collective-permute-start.5 = (bf16[16,2,128,128]{3,2,1,0:T(8,128)(2,1)}, bf16[16,2,128,128]{3,2,1,0:T(8,128)(2,1)S(1)}, u32[]{:S(2)}, u32[]{:S(2)}) collective-permute-start(bf16[16,2,128,128]{3,2,1,0:T(8,128)(2,1)} %get-tuple-element.20), channel_id=1, source_target_pairs={{4,0},{8,4},{12,8},{16,12},{20,16},{24,20},{28,24},{5,1},{9,5},{13... | collective-permute-start | bytes 3145736 | tf_op jit(solution)/shard_map/ppermute | solution.py:32
  209.3 46.2 %collective-permute-start.6 = (bf16[16,2,128,128]{3,2,1,0:T(8,128)(2,1)S(1)}, bf16[16,2,128,128]{3,2,1,0:T(8,128)(2,1)}, u32[]{:S(2)}, u32[]{:S(2)}) collective-permute-start(bf16[16,2,128,128]{3,2,1,0:T(8,128)(2,1)S(1)} %get-tuple-element.21), channel_id=1, source_target_pairs={{0,4},{4,8},{8,12},{12,16},{16,20},{20,24},{24,28},{1,5},{5,9},{9,... | collective-permute-start | bytes 3145736 | tf_op jit(solution)/shard_map/ppermute | solution.py:32
  215.7 19.7 %collective-permute-start.8 = (f32[2,64,128]{2,1,0:T(8,128)S(1)}, f32[2,64,128]{2,1,0:T(8,128)S(1)}, u32[]{:S(2)}, u32[]{:S(2)}) collective-permute-start(f32[2,64,128]{2,1,0:T(8,128)S(1)} %add.91), channel_id=1, source_target_pairs={{0,8},{4,12},{8,0},{12,4},{16,24},{20,28},{24,16},{28,20},{1,9},{5... | collective-permute-start | bytes 196616 | tf_op jit(solution)/shard_map/ppermute | solution.py:9
  235.4 6.0 %collective-permute-start.9 = (f32[2,64,128]{2,1,0:T(8,128)S(1)}, f32[2,64,128]{2,1,0:T(8,128)S(1)}, u32[]{:S(2)}, u32[]{:S(2)}) collective-permute-start(f32[2,64,128]{2,1,0:T(8,128)S(1)} %add.93), channel_id=1, source_target_pairs={{0,16},{4,20},{8,24},{12,28},{16,0},{20,4},{24,8},{28,12},{1,17},{... | collective-permute-start | bytes 196616 | tf_op jit(solution)/shard_map/ppermute | solution.py:9
  244.6 1.0 copy-start.3
  260.1 2.8 copy-start.1
Sparse Core Ops, SparseCore 0:
  217.7 132.0 all-reduce.2
where the time goes:
time: 361 us; the launch traced here: 360 us
  waiting for transfers between devices  157 us (43%)
  other arithmetic  67.9 us (19%)
  local copies, waits for them, and re-layouts  56.5 us (16%)
  matrix products  35.6 us (10%)
  starting transfers between devices  28.3 us (8%)
  between operations  14.3 us (4%)
    psum x1, waiting for transfers between devices, on_device(): grad_near, grad_far = lax.psum((near_term, far_term), ('leaf', 'case'))  83.7 us
    ppermute x6, waiting for transfers between devices, partner(): lax.ppermute(shard, axis, [(i, i ^ 1 << apart) for i in range(lax.axis_si...  63.3 us
    scatter-add x1, other arithmetic, on_device(): landed = jax.ops.segment_sum(contrib, local_ids, num_segments=span_blocks)  56.4 us
    transpose x1, local copies, waits for them, and re-layouts, on_device(): jnp.einsum('bkij,abic->bkajc', kernel_blocks, back_blocks, preferred_elem...  24.7 us
    ppermute x6, starting transfers between devices, partner(): lax.ppermute(shard, axis, [(i, i ^ 1 << apart) for i in range(lax.axis_si...  15.1 us
    gather x2, local copies, waits for them, and re-layouts, on_device(): jnp.take(ext_blocks, local_ids, axis=1)  14.7 us
    dot_general x1, matrix products, on_device(): jnp.einsum('bkij,abic->bkajc', kernel_blocks, back_blocks, preferred_elem...  12.9 us
    ppermute x2, waiting for transfers between devices, shifted(): lax.ppermute(value, axis, [(source, source + steps) for source in range(l...  9.93 us
  transfers between devices with their start and end apart: 11, of which 7 were waited for; matrix products, arithmetic and copies ran while one was open for 34% of the time, Pallas kernels for 0%

commit v1 on v0

--- a/solution.py
+++ b/solution.py
@@ -117,7 +117,7 @@
     far_term = (
         jnp.einsum("arc,ard->cd", exp_bf, projected, preferred_element_type=jnp.float32) * scale
     )
-    grad_near, grad_far = lax.psum((near_term, far_term), ("leaf", "case"))
+    grad_near, grad_far = lax.psum(lax.psum((near_term, far_term), "case"), "leaf")
     return (output, grad_features, grad_near, grad_far)
 
 

time: 361 us -> 332 us (0.920)
  waiting for transfers between devices: 157 us -> 129 us
    ppermute x6, waiting for transfers between devices: 63.3 us -> 45.2 us  [partner(): lax.ppermute(shard, axis, [(i, i ^ 1 << apart) for i in range(lax.axis_si...]
    ppermute x2, waiting for transfers between devices: 9.93 us -> 0.01 us  [shifted(): lax.ppermute(value, axis, [(source, source + steps) for source in range(l...]
    psum x1 -> x2, waiting for transfers between devices: 83.7 us -> 84.2 us  [the longest x1 54.2 us: on_device(): lax.psum(lax.psum((near_term, far_term), 'case'), 'leaf')]
  transfers between devices with their start and end apart: 11 -> 12, of which waited for: 7 -> 6; matrix products, arithmetic and copies ran while one was open for 34% -> 37% of each run, Pallas kernels for 0% -> 0%
where the time goes in v1:
time: 332 us; the launch traced here: 331 us
  waiting for transfers between devices  129 us (39%)
  other arithmetic  69.2 us (21%)
  local copies, waits for them, and re-layouts  54.6 us (16%)
  matrix products  36.5 us (11%)
  starting transfers between devices  27.1 us (8%)
  between operations  14.3 us (4%)
    scatter-add x1, other arithmetic, on_device(): landed = jax.ops.segment_sum(contrib, local_ids, num_segments=span_blocks)  56.5 us
    psum x1, waiting for transfers between devices, on_device(): lax.psum(lax.psum((near_term, far_term), 'case'), 'leaf')  54.2 us
    ppermute x6, waiting for transfers between devices, partner(): lax.ppermute(shard, axis, [(i, i ^ 1 << apart) for i in range(lax.axis_si...  45.2 us
    psum x1, waiting for transfers between devices, on_device(): lax.psum((near_term, far_term), 'case')  30 us
    transpose x1, local copies, waits for them, and re-layouts, on_device(): jnp.einsum('bkij,abic->bkajc', kernel_blocks, back_blocks, preferred_elem...  24.7 us
    gather x2, local copies, waits for them, and re-layouts, on_device(): jnp.take(ext_blocks, local_ids, axis=1)  14.7 us
    ppermute x6, starting transfers between devices, partner(): lax.ppermute(shard, axis, [(i, i ^ 1 << apart) for i in range(lax.axis_si...  13.6 us
    dot_general x1, matrix products, on_device(): jnp.einsum('bkij,abic->bkajc', kernel_blocks, back_blocks, preferred_elem...  13 us
  transfers between devices with their start and end apart: 12, of which 6 were waited for; matrix products, arithmetic and copies ran while one was open for 37% of the time, Pallas kernels for 0%

profile of v1, /device:TPU:0, one launch (start us, length us, event | category | flops | bytes accessed | tf_op | source)
XLA Modules:
  0.0 331.0 jit_solution(9374910898323474554)
XLA Ops:
  7.2 5.1 %collective-permute-start = (bf16[2,2048,128]{2,1,0:T(8,128)(2,1)}, bf16[2,2048,128]{2,1,0:T(8,128)(2,1)S(1)}, u32[]{:S(2)}, u32[]{:S(2)}) collective-permute-start(bf16[2,2048,128]{2,1,0:T(8,128)(2,1)} %param.8), channel_id=1, source_target_pairs={{0,4},{4,8},{8,12},{12,16},{16,20},{20,24},{24,28},{1,5},{5,9},{9,... | collective-permute-start | bytes 3145736 | tf_op jit(solution)/shard_map/ppermute | solution.py:20
  12.3 1.3 collective-permute-start.1
  13.6 1.5 convolution_bitcast_fusion.3
  15.2 2.7 collective-permute-start.2
  17.9 0.7 compare_and_fusion
  18.8 39.9 %collective-permute-done.2 = f32[2,64,128]{2,1,0:T(8,128)S(1)} collective-permute-done((f32[2,64,128]{2,1,0:T(8,128)S(1)}, f32[2,64,128]{2,1,0:T(8,128)S(1)}, u32[]{:S(2)}, u32[]{:S(2)}) %collective-permute-start.2) | collective-permute-done | bytes 65568 | tf_op jit(solution)/shard_map/ppermute | solution.py:9
  58.7 3.5 %collective-permute-start.3 = (f32[2,64,128]{2,1,0:T(8,128)S(1)}, f32[2,64,128]{2,1,0:T(8,128)S(1)}, u32[]{:S(2)}, u32[]{:S(2)}) collective-permute-start(f32[2,64,128]{2,1,0:T(8,128)S(1)} %add.86), channel_id=1, source_target_pairs={{0,8},{4,12},{8,0},{12,4},{16,24},{20,28},{24,16},{28,20},{1,9},{5... | collective-permute-start | bytes 196616 | tf_op jit(solution)/shard_map/ppermute | solution.py:9
  62.3 2.3 collective-permute-done.3
  64.5 3.1 collective-permute-start.4
  67.6 1.0 fusion.50
  68.6 1.3 collective-permute-done.4
  69.9 1.0 fusion.46
  71.1 1.0 copy-done.2
  72.0 2.0 pad_maximum_fusion
  74.0 8.2 %gather_fusion = bf16[192,2,128,128]{3,2,1,0:T(8,128)(2,1)} fusion(bf16[2,48,128,128]{3,2,1,0:T(8,128)(2,1)S(1)} %bitcast.123, s32[1024]{0:T(1024)S(1)} %pad_clamp_fusion), kind=kCustom, calls=%fused_computation | custom fusion | bytes 25166592 | tf_op jit(solution)/shard_map/jit(_take)/gather | solution.py:66
  82.2 6.5 %copy.24 = bf16[2,192,128,128]{3,2,1,0:T(8,128)(2,1)S(1)} copy(bf16[2,192,128,128]{3,2,0,1:T(8,128)(2,1)} %bitcast.124) | data formatting | bytes 25165824 | tf_op jit(solution)/shard_map/jit(_take)/gather | solution.py:66
  88.7 5.5 %fusion.21 = bf16[2,16,128,128]{3,2,0,1:T(8,128)(2,1)} fusion(bf16[16,12,128,128]{3,2,1,0:T(8,128)(2,1)} %param.10, bf16[2,16,12,128,128]{4,3,2,1,0:T(8,128)(2,1)S(1)} %bitcast.125, pred[16,12]{1,0:T(8,128)(4,1)S(1)} %get-tuple-element.20), kind=kOutput, calls=%fused_computation.33 | convolution fusion | flops 1617428480 | bytes 19923136 | tf_op jit(solution)/shard_map/bkij,abkjc->abic/dot_general | solution.py:69
  94.2 1.3 copy.26
  95.6 1.7 fusion.55
  97.3 5.0 %fusion.7 = (bf16[2,2048,128]{2,1,0:T(8,128)(2,1)S(1)}, bf16[2,2048,128]{2,1,0:T(8,128)(2,1)}) fusion(bf16[2,2048,128]{2,1,0:T(8,128)(2,1)} %param.9, f32[2,2048,128]{2,1,0:T(8,128)} %fusion.55, bf16[64,2048]{1,0:T(8,128)(2,1)S(1)} %copy-done, bf16[2,64,128]{2,1,0:T(8,128)(2,1)S(1)} %fusion.34, bf16[128,128]{1,0:T(8,128)(2,1)S(1)} %copy-done.7), kind=kOutput, calls=%fused_computation.19 | convolution fusion | flops 83902464 | bytes 5570560 | tf_op jit(solution)/shard_map/rp,ard->apd/dot_general | solution.py:79
  102.6 1.1 fusion.27
  104.1 0.8 fusion.40
  104.9 1.0 collective-permute-start.7
  105.9 13.0 %convolution_bitcast_fusion = f32[16,12,2,128,128]{3,4,1,2,0:T(8,128)} fusion(bf16[16,12,128,128]{3,2,1,0:T(8,128)(2,1)} %param.10, bf16[2,16,128,128,1]{3,2,1,0,4:T(8,128)(2,1)S(1)} %bitcast.128), kind=kOutput, calls=%fused_computation.5 | convolution fusion | flops 1610612736 | bytes 32505856 | tf_op jit(solution)/shard_map/bkij,abic->bkajc/dot_general | solution.py:98
  118.9 24.7 %copy.29 = f32[16,12,2,128,128]{4,3,2,1,0:T(8,128)} copy(f32[16,12,2,128,128]{3,4,1,2,0:T(8,128)} %convolution_bitcast_fusion) | data formatting | bytes 50331648 | tf_op jit(solution)/shard_map/bkij,abic->bkajc/transpose | solution.py:98
  143.6 3.5 %broadcast_in_dim.15 = f32[48,2,128,128]{3,2,1,0:T(8,128)} broadcast(f32[]{:T(128)} %constant.38.clone.1), dimensions={} | broadcast | bytes 6291460 | tf_op jit(solution)/shard_map/broadcast_in_dim | solution.py:102
  147.0 56.5 %scatter_fusion = f32[48,2,128,128]{3,2,1,0:T(8,128)} fusion(f32[48,2,128,128]{3,2,1,0:T(8,128)} %broadcast_in_dim.15, s32[192]{0:T(256)S(1)} %reshape.77, f32[192,2,128,128]{3,2,1,0:T(8,128)} %bitcast.122), kind=kCustom, calls=%fused_computation.1 | custom fusion | flops 6291456 | bytes 75498240 | tf_op jit(solution)/shard_map/scatter-add | solution.py:102
  203.5 3.5 %convert.4 = bf16[48,2,128,128]{3,2,1,0:T(8,128)(2,1)S(1)} convert(f32[48,2,128,128]{3,2,1,0:T(8,128)} %scatter_fusion) | non-fusion elementwise | flops 1572864 | bytes 9437184 | tf_op jit(solution)/shard_map/convert.1
  207.2 1.3 collective-permute-start.5
  208.5 5.5 %collective-permute-start.6 = (bf16[16,2,128,128]{3,2,1,0:T(8,128)(2,1)S(1)}, bf16[16,2,128,128]{3,2,1,0:T(8,128)(2,1)}, u32[]{:S(2)}, u32[]{:S(2)}) collective-permute-start(bf16[16,2,128,128]{3,2,1,0:T(8,128)(2,1)S(1)} %get-tuple-element.23), channel_id=1, source_target_pairs={{0,4},{4,8},{8,12},{12,16},{16,20},{20,24},{24,28},{1,5},{5,9},{9,... | collective-permute-start | bytes 3145736 | tf_op jit(solution)/shard_map/ppermute | solution.py:32
  214.0 0.8 fusion.26
  215.1 1.5 add.95
  216.6 0.9 collective-permute-start.8
  217.5 30.0 %all-reduce.7.cloned.1.call-done = (f32[128,128]{1,0:T(8,128)}, f32[128,128]{1,0:T(8,128)}) async-done(((f32[128,128]{1,0:T(8,128)}, f32[128,128]{1,0:T(8,128)}), (f32[128,128]{1,0:T(8,128)}, f32[128,128]{1,0:T(8,128)})) %all-reduce.7.cloned.1.call-update) | async-done | bytes 131088 | tf_op jit(solution)/shard_map/psum | solution.py:120
  247.5 0.9 add.97
  248.4 2.5 collective-permute-start.9
  250.8 1.1 fusion.48
  251.9 1.7 collective-permute-done.9
  253.9 1.1 fusion.33
  255.0 1.8 convolution_bitcast_fusion.1
  256.7 2.3 fusion.16
  259.0 2.0 copy.30
  261.0 2.8 reshape.66
  263.9 1.8 add_convert_fusion
  265.7 1.3 copy.35
  267.0 54.2 %all-reduce.5.cloned.1.call-done = (f32[128,128]{1,0:T(8,128)}, f32[128,128]{1,0:T(8,128)}) async-done(((f32[128,128]{1,0:T(8,128)}, f32[128,128]{1,0:T(8,128)}), (f32[128,128]{1,0:T(8,128)}, f32[128,128]{1,0:T(8,128)})) %all-reduce.5.cloned.1.call-update) | async-done | bytes 131088 | tf_op jit(solution)/shard_map/psum | solution.py:120
  321.2 1.5 copy.62
  322.7 1.5 copy.63
  (36 shorter events, 1.9 us)
Async XLA Ops:
  7.2 6.5 %copy-start = (bf16[64,2048]{1,0:T(8,128)(2,1)S(1)}, bf16[64,2048]{1,0:T(8,128)(2,1)}, u32[]{:S(2)}) copy-start(bf16[64,2048]{1,0:T(8,128)(2,1)} %param.12) | copy-start | bytes 786436
  7.2 63.6 %copy-start.3 = (f32[3,64,64]{2,1,0:T(8,128)S(1)}, f32[3,64,64]{2,1,0:T(8,128)}, u32[]{:S(2)}) copy-start(f32[3,64,64]{2,1,0:T(8,128)} %param.15) | copy-start | bytes 147460
  7.2 240.2 %all-reduce.7.cloned.1.call-start = ((), (), s32[]{:S(2)}) async-start(), calls=%async_computation.1 | async-start | bytes 262144 | tf_op jit(solution)/shard_map/psum | solution.py:120
  7.2 63.8 %collective-permute-start = (bf16[2,2048,128]{2,1,0:T(8,128)(2,1)}, bf16[2,2048,128]{2,1,0:T(8,128)(2,1)S(1)}, u32[]{:S(2)}, u32[]{:S(2)}) collective-permute-start(bf16[2,2048,128]{2,1,0:T(8,128)(2,1)} %param.8), channel_id=1, source_target_pairs={{0,4},{4,8},{8,12},{12,16},{16,20},{20,24},{24,28},{1,5},{5,9},{9,... | collective-permute-start | bytes 3145736 | tf_op jit(solution)/shard_map/ppermute | solution.py:20
  12.3 59.7 %collective-permute-start.1 = (bf16[2,2048,128]{2,1,0:T(8,128)(2,1)}, bf16[2,2048,128]{2,1,0:T(8,128)(2,1)}, u32[]{:S(2)}, u32[]{:S(2)}) collective-permute-start(bf16[2,2048,128]{2,1,0:T(8,128)(2,1)} %param.8), channel_id=1, source_target_pairs={{4,0},{8,4},{12,8},{16,12},{20,16},{24,20},{28,24},{5,1},{9,5},{13... | collective-permute-start | bytes 3145736 | tf_op jit(solution)/shard_map/ppermute | solution.py:22
  15.2 43.6 %collective-permute-start.2 = (f32[2,64,128]{2,1,0:T(8,128)S(1)}, f32[2,64,128]{2,1,0:T(8,128)S(1)}, u32[]{:S(2)}, u32[]{:S(2)}) collective-permute-start(f32[2,64,128]{2,1,0:T(8,128)S(1)} %convolution_bitcast_fusion.3), channel_id=1, source_target_pairs={{0,4},{4,0},{8,12},{12,8},{16,20},{20,16},{24,28},{28,24},{1,5},{5... | collective-permute-start | bytes 196616 | tf_op jit(solution)/shard_map/ppermute | solution.py:9
  58.7 5.8 %collective-permute-start.3 = (f32[2,64,128]{2,1,0:T(8,128)S(1)}, f32[2,64,128]{2,1,0:T(8,128)S(1)}, u32[]{:S(2)}, u32[]{:S(2)}) collective-permute-start(f32[2,64,128]{2,1,0:T(8,128)S(1)} %add.86), channel_id=1, source_target_pairs={{0,8},{4,12},{8,0},{12,4},{16,24},{20,28},{24,16},{28,20},{1,9},{5... | collective-permute-start | bytes 196616 | tf_op jit(solution)/shard_map/ppermute | solution.py:9
  64.5 5.3 %collective-permute-start.4 = (f32[2,64,128]{2,1,0:T(8,128)S(1)}, f32[2,64,128]{2,1,0:T(8,128)S(1)}, u32[]{:S(2)}, u32[]{:S(2)}) collective-permute-start(f32[2,64,128]{2,1,0:T(8,128)S(1)} %add.88), channel_id=1, source_target_pairs={{0,16},{4,20},{8,24},{12,28},{16,0},{20,4},{24,8},{28,12},{1,17},{... | collective-permute-start | bytes 196616 | tf_op jit(solution)/shard_map/ppermute | solution.py:9
  71.0 26.3 %copy-start.5 = (bf16[2,64,128]{2,1,0:T(8,128)(2,1)}, bf16[2,64,128]{2,1,0:T(8,128)(2,1)S(1)}, u32[]{:S(2)}) copy-start(bf16[2,64,128]{2,1,0:T(8,128)(2,1)S(1)} %fusion.34) | copy-start | bytes 98308
  71.1 1.0 copy-start.2
  94.2 1.3 copy-start.4
  95.5 1.8 copy-start.7
  104.9 110.2 %collective-permute-start.7 = (f32[2,64,128]{2,1,0:T(8,128)}, f32[2,64,128]{2,1,0:T(8,128)}, u32[]{:S(2)}, u32[]{:S(2)}) collective-permute-start(f32[2,64,128]{2,1,0:T(8,128)} %fusion.40), channel_id=1, source_target_pairs={{0,4},{4,0},{8,12},{12,8},{16,20},{20,16},{24,28},{28,24},{1,5},{5... | collective-permute-start | bytes 196616 | tf_op jit(solution)/shard_map/ppermute | solution.py:9
  207.0 7.0 %copy-start.6 = (bf16[2,64,128]{2,1,0:T(8,128)(2,1)S(1)}, bf16[2,64,128]{2,1,0:T(8,128)(2,1)}, u32[]{:S(2)}) copy-start(bf16[2,64,128]{2,1,0:T(8,128)(2,1)} %copy-done.5) | copy-start | bytes 98308
  207.2 49.6 %collective-permute-start.5 = (bf16[16,2,128,128]{3,2,1,0:T(8,128)(2,1)S(1)}, bf16[16,2,128,128]{3,2,1,0:T(8,128)(2,1)S(1)}, u32[]{:S(2)}, u32[]{:S(2)}) collective-permute-start(bf16[16,2,128,128]{3,2,1,0:T(8,128)(2,1)S(1)} %get-tuple-element.22), channel_id=1, source_target_pairs={{4,0},{8,4},{12,8},{16,12},{20,16},{24,20},{28,24},{5,1},{9,5},{13... | collective-permute-start | bytes 3145736 | tf_op jit(solution)/shard_map/ppermute | solution.py:32
  208.5 48.3 %collective-permute-start.6 = (bf16[16,2,128,128]{3,2,1,0:T(8,128)(2,1)S(1)}, bf16[16,2,128,128]{3,2,1,0:T(8,128)(2,1)}, u32[]{:S(2)}, u32[]{:S(2)}) collective-permute-start(bf16[16,2,128,128]{3,2,1,0:T(8,128)(2,1)S(1)} %get-tuple-element.23), channel_id=1, source_target_pairs={{0,4},{4,8},{8,12},{12,16},{16,20},{20,24},{24,28},{1,5},{5,9},{9,... | collective-permute-start | bytes 3145736 | tf_op jit(solution)/shard_map/ppermute | solution.py:32
  214.9 106.4 %all-reduce.5.cloned.1.call-start = ((), (), s32[]{:S(2)}) async-start(), calls=%async_computation | async-start | bytes 262144 | tf_op jit(solution)/shard_map/psum | solution.py:120
  216.6 30.9 %collective-permute-start.8 = (f32[2,64,128]{2,1,0:T(8,128)}, f32[2,64,128]{2,1,0:T(8,128)}, u32[]{:S(2)}, u32[]{:S(2)}) collective-permute-start(f32[2,64,128]{2,1,0:T(8,128)} %add.95), channel_id=1, source_target_pairs={{0,8},{4,12},{8,0},{12,4},{16,24},{20,28},{24,16},{28,20},{1,9},{5... | collective-permute-start | bytes 196616 | tf_op jit(solution)/shard_map/ppermute | solution.py:9
  248.4 5.2 %collective-permute-start.9 = (f32[2,64,128]{2,1,0:T(8,128)S(1)}, f32[2,64,128]{2,1,0:T(8,128)S(1)}, u32[]{:S(2)}, u32[]{:S(2)}) collective-permute-start(f32[2,64,128]{2,1,0:T(8,128)S(1)} %add.97), channel_id=1, source_target_pairs={{0,16},{4,20},{8,24},{12,28},{16,0},{20,4},{24,8},{28,12},{1,17},{... | collective-permute-start | bytes 196616 | tf_op jit(solution)/shard_map/ppermute | solution.py:9
  261.0 2.8 copy-start.1
Sparse Core Ops, SparseCore 0:
  215.0 32.4 all-reduce.6
  251.3 69.8 all-reduce.4
